TPU v7x, 32 devices: a whole 2x2x4 slice. The times are simulated.
32 devices in a mesh: row: 2 (over core), col: 2 (over x), seq: 8 (over z, y).
Axes of the slice: x: 2, y: 2, z: 4, core: 2. Of those that a mesh axis runs over, the one named last changes fastest.
Arguments:
- states: bfloat16 [128, 4, 5120], P('col', None, 'row'), may hold values from -64 to 64
- norm_gain: float32 [5120], P('row'), may hold values from 0.1 to 1.9
- wq: bfloat16 [5120, 4096], P('row', 'col'), may hold values from -0.078125 to 0.078125
- wk: bfloat16 [5120, 1024], P('row', 'col'), may hold values from -0.21875 to 0.21875
- wv: bfloat16 [5120, 1024], P('row', 'col'), may hold values from -0.078125 to 0.078125
- wo: bfloat16 [4096, 5120], P('col', 'row'), may hold values from -0.09375 to 0.09375
- lengths: int32 [128], P('row'), may hold values from 1 to 8192, as said below
- slot_request: int32 [800], P(('row', 'seq')), may hold values from 0 to 64, as said below
- slot_block_number: int32 [800], P(('row', 'seq')), may hold values from 0 to 63, as said below
- paged_key_cache: bfloat16 [800, 128, 1024], P(('row', 'seq'), None, 'col'), may hold values from -120 to 120
- paged_value_cache: bfloat16 [800, 128, 1024], P(('row', 'seq'), None, 'col'), may hold values from -6 to 6
Outputs:
- attended: bfloat16 [128, 4, 5120], P('col', None, 'row')
- new_keys: bfloat16 [128, 4, 1024], P('row', None, 'col')
- new_values: bfloat16 [128, 4, 1024], P('row', None, 'col')
Inputs may be any that keep to these rules, and one draw needn't show every extreme that they name: `lengths`: within every 64 consecutive requests, 8 have exactly 8192 cached tokens and the others fewer than 128. `slot_request`: each request's block 0 and every block that holds a position visible to one of its steps stand in exactly one slot of its index of row; a long request has exactly 33 slots. 64 marks an empty slot; every index of row has empty slots. `slot_block_number`: 0 in empty slots.
All inputs are finite; a program needn't handle non-finite values.
Results may differ from a plain program's by a relative error of at most 0.034.
Values may be sent and summed in bfloat16 or wider, within the bound.
No kernel may reach another device: no remote copies, remote signals or barrier semaphores. Data moves between devices by JAX's collectives and lax.ppermute only.
A program may use at most 192 MiB of HBM per device.

v0:
```python
import math
import jax
import jax.numpy as jnp
from jax import lax
from jax.sharding import PartitionSpec as P

D = 5120
HEAD_SIZE = 128
WINDOW = 4096
SINK = 4
QUERY_PER_KEY = 4
EPSILON = 1e-05
NEGATIVE_FILL = -1e30
ROPE_BASE = 100000000.0


def rotary_apply(values, token_positions):
    half_dim = values.shape[-1] // 2
    frequency = ROPE_BASE ** (-(jnp.arange(half_dim, dtype=jnp.float32) * 2.0 / values.shape[-1]))
    angles = (token_positions.astype(jnp.float32)[..., None] * frequency)[..., None, :]
    cosine = jnp.cos(angles)
    sine_part = jnp.sin(angles)
    lower = values[..., :half_dim]
    upper = values[..., half_dim:]
    return jnp.concatenate(
        [lower * cosine - upper * sine_part, upper * cosine + lower * sine_part], -1
    )


def slot_parts(query_rows, lengths, slot_request, slot_block_number, key_rows, value_rows):
    req_count = query_rows.shape[0]
    step_count = query_rows.shape[1]
    block_len = key_rows.shape[1]
    picked = jnp.minimum(slot_request, req_count - 1)
    in_use = slot_request < req_count
    slot_queries = query_rows[picked]
    scores = jnp.einsum(
        "nsagh,nbah->nasgb", slot_queries, key_rows, preferred_element_type=jnp.float32
    ) * (1.0 / math.sqrt(HEAD_SIZE))
    key_pos = (
        slot_block_number[:, None] * block_len + jnp.arange(block_len, dtype=jnp.int32)[None, :]
    )
    own_len = lengths[picked]
    query_pos = own_len[:, None] + jnp.arange(step_count, dtype=jnp.int32)[None, :]
    visible = (
        in_use[:, None, None]
        & (key_pos[:, None, :] < own_len[:, None, None])
        & ((key_pos[:, None, :] < SINK) | (key_pos[:, None, :] > query_pos[:, :, None] - WINDOW))
    )
    visible = visible[:, None, :, None, :]
    slot_peak = jnp.max(jnp.where(visible, scores, NEGATIVE_FILL), -1)
    weights = jnp.where(visible, jnp.exp(scores - slot_peak[..., None]), 0.0)
    slot_total = jnp.sum(weights, -1)
    slot_acc = jnp.einsum(
        "nasgb,nbah->nasgh",
        weights.astype(jnp.bfloat16),
        value_rows,
        preferred_element_type=jnp.float32,
    )
    member = slot_request[None, :] == jnp.arange(req_count, dtype=jnp.int32)[:, None]
    local_peak = jnp.max(
        jnp.where(member[:, :, None, None, None], slot_peak[None], NEGATIVE_FILL), 1
    )
    return (local_peak, (slot_peak, slot_total, slot_acc, member, picked))


def pool_sums(held, running_peak):
    slot_peak, slot_total, slot_acc, member, picked = held
    factor = jnp.exp(slot_peak - running_peak[picked])
    as_member = member.astype(jnp.float32)
    running_totals = jnp.einsum(
        "rn,nasg->rasg", as_member, slot_total * factor, precision=lax.Precision.HIGHEST
    )
    weighted_values = jnp.einsum(
        "rn,nasgh->rasgh", as_member, slot_acc * factor[..., None], precision=lax.Precision.HIGHEST
    )
    return (running_totals, weighted_values)


def fresh_part(query_rows, key_all, value_all):
    step_count = query_rows.shape[1]
    used = key_all.shape[1]
    scores = jnp.einsum(
        "rsagh,ruah->rasgu", query_rows, key_all, preferred_element_type=jnp.float32
    ) * (1.0 / math.sqrt(HEAD_SIZE))
    causal = (
        jnp.arange(used, dtype=jnp.int32)[None, :]
        <= jnp.arange(step_count, dtype=jnp.int32)[:, None]
    )
    causal = causal[None, None, :, None, :]
    running_peak = jnp.max(jnp.where(causal, scores, NEGATIVE_FILL), -1)
    weights = jnp.where(causal, jnp.exp(scores - running_peak[..., None]), 0.0)
    running_totals = jnp.sum(weights, -1)
    weighted_values = jnp.einsum(
        "rasgu,ruah->rasgh",
        weights.astype(jnp.bfloat16),
        value_all,
        preferred_element_type=jnp.float32,
    )
    return (running_peak, running_totals, weighted_values)


def merge_parts(earlier, later):
    running_peak = jnp.maximum(earlier[0], later[0])
    first_factor = jnp.exp(earlier[0] - running_peak)
    second_factor = jnp.exp(later[0] - running_peak)
    running_totals = earlier[1] * first_factor + later[1] * second_factor
    weighted_values = earlier[2] * first_factor[..., None] + later[2] * second_factor[..., None]
    return (running_peak, running_totals, weighted_values)


def on_device(
    states,
    norm_gain,
    wq,
    wk,
    wv,
    wo,
    lengths,
    slot_request,
    slot_block_number,
    paged_key_cache,
    paged_value_cache,
):
    q_width = wq.shape[1]
    k_width = wk.shape[1]
    heads_kv = k_width // HEAD_SIZE
    req_count = lengths.shape[0]
    block_len = paged_key_cache.shape[1]
    key_rows = paged_key_cache.reshape(paged_key_cache.shape[0], block_len, heads_kv, HEAD_SIZE)
    value_rows = paged_value_cache.reshape(
        paged_value_cache.shape[0], block_len, heads_kv, HEAD_SIZE
    )
    step_count = states.shape[1]
    as_float = states.astype(jnp.float32)
    squares = lax.psum(jnp.sum(as_float * as_float, -1), "row")
    normed = (as_float * lax.rsqrt(squares / D + EPSILON)[..., None] * norm_gain).astype(
        jnp.bfloat16
    )
    gathered = lax.all_gather(normed, "col", axis=0, tiled=True)
    piece_rows = gathered.reshape(req_count * lax.axis_size("row") * step_count, -1)
    parts_out = [
        jnp.dot(piece_rows, matrix, preferred_element_type=jnp.float32) for matrix in (wq, wk, wv)
    ]
    output_projected = lax.psum_scatter(
        jnp.concatenate(parts_out, axis=-1)
        .reshape(req_count * lax.axis_size("row"), step_count, -1)
        .astype(jnp.bfloat16),
        "row",
        scatter_dimension=0,
        tiled=True,
    ).astype(jnp.float32)
    token_positions = lengths[:, None] + jnp.arange(step_count, dtype=jnp.int32)[None, :]
    query_rows = rotary_apply(
        output_projected[..., :q_width].reshape(req_count, step_count, -1, HEAD_SIZE),
        token_positions,
    ).astype(jnp.bfloat16)
    query_rows = query_rows.reshape(req_count, step_count, heads_kv, QUERY_PER_KEY, HEAD_SIZE)
    current_key = rotary_apply(
        output_projected[..., q_width : q_width + k_width].reshape(
            req_count, step_count, heads_kv, HEAD_SIZE
        ),
        token_positions,
    ).astype(jnp.bfloat16)
    current_value = (
        output_projected[..., q_width + k_width :]
        .reshape(req_count, step_count, heads_kv, HEAD_SIZE)
        .astype(jnp.bfloat16)
    )
    local_peak, held = slot_parts(
        query_rows, lengths, slot_request, slot_block_number, key_rows, value_rows
    )
    running_peak = lax.pmax(local_peak, "seq")
    running_totals, weighted_values = pool_sums(held, running_peak)
    running_totals, weighted_values = (
        lax.psum(running_totals.astype(jnp.bfloat16), "seq").astype(jnp.float32),
        lax.psum(weighted_values.astype(jnp.bfloat16), "seq").astype(jnp.float32),
    )
    fresh = fresh_part(query_rows, current_key, current_value)
    running_peak, running_totals, weighted_values = merge_parts(
        (running_peak, running_totals, weighted_values), fresh
    )
    heads_out = (
        (weighted_values / running_totals[..., None])
        .transpose(0, 2, 1, 3, 4)
        .reshape(req_count, step_count, -1)
        .astype(jnp.bfloat16)
    )
    piece_rows = lax.all_gather(heads_out, "row", axis=0, tiled=True)
    row_count = piece_rows.shape[0]
    product = jnp.dot(
        piece_rows.reshape(row_count * step_count, -1), wo, preferred_element_type=jnp.float32
    )
    partials = product.reshape(row_count, step_count, -1)
    attended = lax.psum_scatter(
        partials.astype(jnp.bfloat16), "col", scatter_dimension=0, tiled=True
    )
    return (
        attended,
        current_key.reshape(req_count, step_count, k_width),
        current_value.reshape(req_count, step_count, k_width),
    )


def solution(mesh):
    in_specs = (
        P("col", None, "row"),
        P("row"),
        P("row", "col"),
        P("row", "col"),
        P("row", "col"),
        P("col", "row"),
        P("row"),
        P(("row", "seq")),
        P(("row", "seq")),
        P(("row", "seq"), None, "col"),
        P(("row", "seq"), None, "col"),
    )
    out_specs = (P("col", None, "row"), P("row", None, "col"), P("row", None, "col"))
    return jax.shard_map(
        on_device, mesh=mesh, in_specs=in_specs, out_specs=out_specs, check_vma=False
    )
```

profile of v0, /device:TPU:0, one launch (start us, length us, event | category | flops | bytes accessed | tf_op | source)
XLA Modules:
  0.0 341.6 jit_solution(11022406717256435798)
XLA Ops:
  7.2 2.2 fusion.9
  9.5 2.6 psum.21
  12.2 3.1 fusion.11
  15.4 41.7 %all-gather.3.cloned.1.call-done = bf16[128,4,2560]{2,1,0:T(4,128)(2,1)} async-done(((bf16[64,4,2560]{2,1,0:T(4,128)(2,1)}), bf16[128,4,2560]{2,1,0:T(4,128)(2,1)}) %all-gather.3.cloned.1.call-update) | async-done | bytes 2621456 | tf_op jit(solution)/shard_map/all_gather | solution.py:140
  57.1 5.3 %reshape.218 = bf16[512,2560]{1,0:T(8,128)(2,1)} reshape(bf16[128,4,2560]{2,1,0:T(4,128)(2,1)} %all-gather.3.cloned.1.call-done) | data formatting | bytes 5242880 | tf_op jit(solution)/shard_map/reshape | solution.py:141
  62.5 3.4 convolution_convert_fusion.1
  67.4 8.5 %convolution_convert_fusion = bf16[512,2048]{1,0:T(8,128)(2,1)S(1)} fusion(bf16[512,2560]{1,0:T(8,128)(2,1)S(1)} %copy-done.4, bf16[2560,2048]{1,0:T(8,128)(2,1)} %param.13), kind=kOutput, calls=%fused_computation.13 | convolution fusion | flops 5369757696 | bytes 15204352 | tf_op jit(solution)/shard_map/dot_general | solution.py:143
  76.2 2.7 convert_element_type.70
  81.8 12.3 %reshape.220 = bf16[50,128,4,128]{3,2,1,0:T(4,128)(2,1)} reshape(bf16[50,128,512]{2,1,0:T(8,128)(2,1)} %param.20) | data formatting | bytes 13107200 | tf_op jit(solution)/shard_map/reshape | solution.py:130
  94.1 12.4 %reshape.221 = bf16[50,128,4,128]{3,2,1,0:T(4,128)(2,1)} reshape(bf16[50,128,512]{2,1,0:T(8,128)(2,1)} %param.21) | data formatting | bytes 13107200 | tf_op jit(solution)/shard_map/reshape | solution.py:131
  114.8 2.4 reshape.258
  122.8 10.3 %fusion.33 = f32[64,4,4,4,4]{3,4,2,1,0:T(4,128)S(1)} fusion(bf16[64,4,4,4,128]{4,3,2,0,1:T(4,128)(2,1)S(1)} %pad_maximum_fusion.1, bf16[64,4,4,64]{3,1,2,0:T(4,128)(2,1)} %get-tuple-element.34, bf16[64,4,4,64]{3,1,2,0:T(4,128)(2,1)S(1)} %get-tuple-element.33), kind=kOutput, calls=%fused_computation.49 | convolution fusion | flops 4718592 | bytes 1376256 | tf_op jit(solution)/shard_map/rsagh,ruah->rasgu/dot_general | solution.py:83
  134.8 6.8 %select_reduce_fusion.1 = (f32[50,4,4,4]{3,2,1,0:T(4,128)S(1)}, f32[50,4,4,4,128]{4,3,2,1,0:T(4,128)S(1)}) fusion(pred[50,4,128]{2,1,0:T(4,128)(4,1)S(1)} %or_and_fusion, bf16[50,4,4,4,128]{4,3,1,2,0:T(4,128)(2,1)} %gather_fusion.1, bf16[50,128,4,128,1]{3,2,1,0,4:T(4,128)(2,1)} %bitcast.60), kind=kOutput, calls=%fused_computation.27 | convolution fusion | flops 106083200 | bytes 9049600 | tf_op jit(solution)/shard_map/nsagh,nbah->nasgb/dot_general | solution.py:37
  142.7 37.1 %pmax.7 = f32[64,4,4,4]{0,3,2,1:T(4,128)S(1)} all-reduce(f32[64,4,4,4]{0,3,2,1:T(4,128)S(1)} %select_reduce_fusion), channel_id=1, replica_groups=mesh['row'=2,'col'=2,'seq'=8] {'seq'}, use_global_device_ids=true, to_apply=%region_5.6 | all-reduce | flops 4096 | bytes 32768 | tf_op jit(solution)/shard_map/pmax | solution.py:173
  179.8 2.7 fusion.24
  183.9 4.5 %fusion.20 = f32[50,4,4,4,128]{4,3,2,1,0:T(4,128)S(1)} fusion(bf16[50,128,4,128,1]{3,2,1,0,4:T(4,128)(2,1)} %bitcast.59, f32[50,4,4,4,128]{4,3,2,1,0:T(4,128)S(1)} %get-tuple-element.42, f32[50,4,4,4]{3,2,1,0:T(4,128)S(1)} %bitcast.67, f32[50,4,4,4]{3,2,1,0:T(4,128)S(1)} %get-tuple-element.41, pred[50,4,128]{2,1,0:T(4,128)(4,1)} %copy-done.9), kind=kOutput, calls=%fused_computation.30 | convolution fusion | flops 106905600 | bytes 9881600 | tf_op jit(solution)/shard_map/nasgb,nbah->nasgh/dot_general | solution.py:54
  188.5 3.2 fusion.17
  196.5 33.6 %psum.23 = bf16[64,4,4,4]{0,3,2,1:T(4,128)(2,1)S(1)} all-reduce(bf16[64,4,4,4]{0,3,2,1:T(4,128)(2,1)S(1)} %convert_element_type.80), channel_id=1, replica_groups=mesh['row'=2,'col'=2,'seq'=8] {'seq'}, use_global_device_ids=true, to_apply=%region_9.10 | all-reduce | flops 4096 | bytes 16384 | tf_op jit(solution)/shard_map/psum | solution.py:176
  230.7 35.7 %all-reduce.4.cloned.1.call-done = bf16[64,4,4,4,128]{4,0,3,2,1:T(8,128)(2,1)} async-done(((bf16[64,4,4,4,128]{4,0,3,2,1:T(8,128)(2,1)}), bf16[64,4,4,4,128]{4,0,3,2,1:T(8,128)(2,1)}) %all-reduce.4.cloned.1.call-update) | async-done | bytes 1048592 | tf_op jit(solution)/shard_map/psum | solution.py:177
  266.3 3.4 fusion.23
  272.2 10.3 %all-gather.5.cloned.1.call-done = bf16[128,4,2048]{2,0,1:T(8,128)(2,1)} async-done(((bf16[64,4,2048]{2,0,1:T(8,128)(2,1)}), bf16[128,4,2048]{2,0,1:T(8,128)(2,1)}) %all-gather.5.cloned.1.call-update) | async-done | bytes 2097168 | tf_op jit(solution)/shard_map/all_gather | solution.py:189
  282.5 10.0 %fusion.6 = bf16[128,4,2560]{2,0,1:T(8,128)(2,1)} fusion(bf16[128,4,2048]{2,0,1:T(8,128)(2,1)} %all-gather.5.cloned.1.call-done, bf16[2048,2560]{1,0:T(8,128)(2,1)} %param.16), kind=kOutput, calls=%fused_computation.9 | convolution fusion | flops 5370019840 | bytes 15204352 | tf_op jit(solution)/shard_map/dot_general | solution.py:191
  294.6 36.9 %reduce-scatter.2.cloned.1.call-done = bf16[64,4,2560]{2,0,1:T(8,128)(2,1)} async-done(((bf16[128,4,2560]{2,0,1:T(8,128)(2,1)}), bf16[64,4,2560]{2,0,1:T(8,128)(2,1)}) %reduce-scatter.2.cloned.1.call-update) | async-done | bytes 1310736 | tf_op jit(solution)/shard_map/reduce_scatter | solution.py:195
  331.5 3.4 copy.155
  (95 shorter events, 32.1 us)
Async XLA Ops:
  7.2 55.3 %copy-start = (bf16[2560,512]{1,0:T(8,128)(2,1)S(1)}, bf16[2560,512]{1,0:T(8,128)(2,1)}, u32[]{:S(2)}) copy-start(bf16[2560,512]{1,0:T(8,128)(2,1)} %param.15) | copy-start | bytes 7864324
  7.2 50.0 %all-gather.3.cloned.1.call-start = ((), (), s32[]{:S(2)}) async-start(), calls=%async_computation.1 | async-start | bytes 3932160 | tf_op jit(solution)/shard_map/all_gather | solution.py:140
  15.4 94.1 %all-reduce.6.cloned.1.call-start = ((), (), s32[]{:S(2)}) async-start(), calls=%async_computation.5 | async-start | bytes 6291456
  62.5 3.4 %copy-start.4 = (bf16[512,2560]{1,0:T(8,128)(2,1)S(1)}, bf16[512,2560]{1,0:T(8,128)(2,1)}, u32[]{:S(2)}) copy-start(bf16[512,2560]{1,0:T(8,128)(2,1)} %reshape.218) | copy-start | bytes 7864324
  62.5 3.4 %copy-start.15 = (bf16[2560,512]{1,0:T(8,128)(2,1)S(1)}, bf16[2560,512]{1,0:T(8,128)(2,1)}, u32[]{:S(2)}) copy-start(bf16[2560,512]{1,0:T(8,128)(2,1)} %param.14) | copy-start | bytes 7864324
  78.9 0.7 copy-start.12
  78.9 0.7 copy-start.2
  78.9 187.4 %all-reduce.4.cloned.1.call-start = ((), (), s32[]{:S(2)}) async-start(), calls=%async_computation.2 | async-start | bytes 2097152 | tf_op jit(solution)/shard_map/psum | solution.py:177
  79.6 41.0 %copy-start.11 = (s32[1024]{0:T(1024)}, s32[1024]{0:T(1024)S(1)}, u32[]{:S(2)}) copy-start(s32[1024]{0:T(1024)S(1)} %pad_clamp_fusion) | copy-start | bytes 12292
  94.1 12.4 %copy-start.17 = (u32[32]{0:T(128)S(1)}, u32[32]{0:T(128)}, u32[]{:S(2)}) copy-start(u32[32]{0:T(128)} %constant.40) | copy-start | bytes 388
  94.1 14.2 %copy-start.16 = (s32[50]{0:T(128)S(1)}, s32[50]{0:T(128)}, u32[]{:S(2)}) copy-start(s32[50]{0:T(128)} %param.19) | copy-start | bytes 604
  109.4 25.4 %copy-start.9 = (pred[50,4,128]{2,1,0:T(4,128)(4,1)}, pred[50,4,128]{2,1,0:T(4,128)(4,1)S(1)}, u32[]{:S(2)}) copy-start(pred[50,4,128]{2,1,0:T(4,128)(4,1)S(1)} %or_and_fusion) | copy-start | bytes 76804
  111.3 2.3 copy-start.3
  114.8 8.0 %copy-start.5 = (bf16[64,4,4,64]{3,1,2,0:T(4,128)(2,1)}, bf16[64,4,4,64]{3,1,2,0:T(4,128)(2,1)S(1)}, u32[]{:S(2)}) copy-start(bf16[64,4,4,64]{3,1,2,0:T(4,128)(2,1)S(1)} %get-tuple-element.33) | copy-start | bytes 393220
  134.8 6.9 %copy-start.10 = (pred[64,50]{0,1:T(8,128)(4,1)S(1)}, pred[64,50]{0,1:T(8,128)(4,1)}, u32[]{:S(2)}) copy-start(pred[64,50]{0,1:T(8,128)(4,1)} %iota_compare_fusion) | copy-start | bytes 9604
  183.9 4.6 %copy-start.13 = (s32[50]{0:T(128)S(1)}, s32[50]{0:T(128)}, u32[]{:S(2)}) copy-start(s32[50]{0:T(128)} %param.18) | copy-start | bytes 604
  188.5 3.3 copy-start.14
  191.7 90.8 %all-gather.5.cloned.1.call-start = ((), (), s32[]{:S(2)}) async-start(), calls=%async_computation.3 | async-start | bytes 3145728 | tf_op jit(solution)/shard_map/all_gather | solution.py:189
  194.0 36.1 %copy-start.8 = (bf16[64,4,512]{2,1,0:T(4,128)(2,1)S(1)}, bf16[64,4,512]{2,1,0:T(4,128)(2,1)}, u32[]{:S(2)}) copy-start(bf16[64,4,512]{2,1,0:T(4,128)(2,1)} %slice.47) | copy-start | bytes 786436
  272.2 59.3 %reduce-scatter.2.cloned.1.call-start = ((), (), s32[]{:S(2)}) async-start(), calls=%async_computation.4 | async-start | bytes 3932160 | tf_op jit(solution)/shard_map/reduce_scatter | solution.py:195
  292.6 0.9 copy-start.6
  292.6 1.0 copy-start.7
  293.6 41.3 %copy-start.1 = (bf16[2560,512]{1,0:T(8,128)(2,1)S(1)}, bf16[2560,512]{1,0:T(8,128)(2,1)}, u32[]{:S(2)}) copy-start(bf16[2560,512]{1,0:T(8,128)(2,1)} %param.15) | copy-start | bytes 7864324
Sparse Core Ops, SparseCore 0:
  15.5 41.5 all-gather.2
  79.0 23.2 all-reduce.5
  191.8 74.4 all-reduce.3
  272.3 10.1 all-gather.4
  292.7 38.7 reduce-scatter.1
where the time goes:
time: 348 us; the launch traced here: 342 us
  waiting for transfers between devices  125 us (36%)
  blocking collectives  73.2 us (21%)
  local copies, waits for them, and re-layouts  57 us (16%)
  matrix products  49.1 us (14%)
  other arithmetic  22.5 us (6%)
  between operations  15 us (4%)
    all_gather x1, waiting for transfers between devices, on_device(): gathered = lax.all_gather(normed, 'col', axis=0, tiled=True)  41.7 us
    pmax x1, blocking collectives, on_device(): running_peak = lax.pmax(local_peak, 'seq')  37.1 us
    reduce_scatter x1, waiting for transfers between devices, on_device(): lax.psum_scatter(partials.astype(jnp.bfloat16), 'col', scatter_dimension=...  36.9 us
    psum x1, waiting for transfers between devices, on_device(): lax.psum(weighted_values.astype(jnp.bfloat16), 'seq').astype(jnp.float32)  35.7 us
    psum x1, blocking collectives, on_device(): lax.psum(running_totals.astype(jnp.bfloat16), 'seq').astype(jnp.float32)  33.6 us
    dot_general x3, matrix products, on_device(): jnp.dot(piece_rows, matrix, preferred_element_type=jnp.float32)  13.4 us
    reshape x1, local copies, waits for them, and re-layouts, on_device(): paged_value_cache.reshape(paged_value_cache.shape[0], block_len, heads_kv...  12.4 us
    reshape x1, local copies, waits for them, and re-layouts, on_device(): paged_key_cache.reshape(paged_key_cache.shape[0], block_len, heads_kv, HE...  12.3 us
  transfers between devices with their start and end apart: 5, of which 4 were waited for; matrix products, arithmetic and copies ran while one was open for 10% of the time, Pallas kernels for 0%

commit v1 on v0

--- a/solution.py
+++ b/solution.py
@@ -174,7 +174,9 @@
     running_totals, weighted_values = pool_sums(held, running_peak)
     running_totals, weighted_values = (
         lax.psum(running_totals.astype(jnp.bfloat16), "seq").astype(jnp.float32),
-        lax.psum(weighted_values.astype(jnp.bfloat16), "seq").astype(jnp.float32),
+        jnp.sum(lax.all_gather(weighted_values.astype(jnp.bfloat16), "seq"), axis=0).astype(
+            jnp.float32
+        ),
     )
     fresh = fresh_part(query_rows, current_key, current_value)
     running_peak, running_totals, weighted_values = merge_parts(

time: 348 us -> 398 us (1.14)
  waiting for transfers between devices: 125 us -> 156 us
  blocking collectives: 73.2 us -> 85.6 us
    all_gather x0 -> x1, waiting for transfers between devices: none -> 68.4 us  [on_device(): lax.all_gather(weighted_values.astype(jnp.bfloat16), 'seq')]
    psum x1 -> x0, waiting for transfers between devices: 35.7 us -> none  [on_device(): lax.psum(weighted_values.astype(jnp.bfloat16), 'seq').astype(jnp.float32)]
    pmax x1, blocking collectives: 37.1 us -> 49.1 us  [on_device(): running_peak = lax.pmax(local_peak, 'seq')]
    reduce_sum x0 -> x2, other arithmetic: none -> 5.84 us  [the longest x1 5.65 us: on_device(): jnp.sum(lax.all_gather(weighted_values.astype(jnp.bfloat16), 'seq'), axis=0)]
    unnamed x38 -> x52, local copies, waits for them, and re-layouts: 6.14 us -> 8.33 us
  transfers between devices with their start and end apart: 5 -> 5, of which waited for: 4 -> 4; matrix products, arithmetic and copies ran while one was open for 10% -> 12% of each run, Pallas kernels for 0% -> 0%
where the time goes in v1:
time: 398 us; the launch traced here: 392 us
  waiting for transfers between devices  156 us (39%)
  blocking collectives  85.6 us (22%)
  local copies, waits for them, and re-layouts  59.4 us (15%)
  matrix products  49.3 us (12%)
  other arithmetic  26.1 us (7%)
  between operations  15.1 us (4%)
    all_gather x1, waiting for transfers between devices, on_device(): lax.all_gather(weighted_values.astype(jnp.bfloat16), 'seq')  68.4 us
    pmax x1, blocking collectives, on_device(): running_peak = lax.pmax(local_peak, 'seq')  49.1 us
    all_gather x1, waiting for transfers between devices, on_device(): gathered = lax.all_gather(normed, 'col', axis=0, tiled=True)  41.7 us
    reduce_scatter x1, waiting for transfers between devices, on_device(): lax.psum_scatter(partials.astype(jnp.bfloat16), 'col', scatter_dimension=...  36.8 us
    psum x1, blocking collectives, on_device(): lax.psum(running_totals.astype(jnp.bfloat16), 'seq').astype(jnp.float32)  33.9 us
    dot_general x3, matrix products, on_device(): jnp.dot(piece_rows, matrix, preferred_element_type=jnp.float32)  13.4 us
    reshape x1, local copies, waits for them, and re-layouts, on_device(): paged_value_cache.reshape(paged_value_cache.shape[0], block_len, heads_kv...  12.4 us
    reshape x1, local copies, waits for them, and re-layouts, on_device(): paged_key_cache.reshape(paged_key_cache.shape[0], block_len, heads_kv, HE...  12.3 us
  transfers between devices with their start and end apart: 5, of which 4 were waited for; matrix products, arithmetic and copies ran while one was open for 12% of the time, Pallas kernels for 0%

profile of v1, /device:TPU:0, one launch (start us, length us, event | category | flops | bytes accessed | tf_op | source)
XLA Modules:
  0.0 392.0 jit_solution(11985815563443540572)
XLA Ops:
  7.2 2.2 fusion.9
  9.5 2.6 psum.14
  12.2 3.1 fusion.11
  15.4 41.7 %all-gather.5.cloned.1.call-done = bf16[128,4,2560]{2,1,0:T(4,128)(2,1)} async-done(((bf16[64,4,2560]{2,1,0:T(4,128)(2,1)}), bf16[128,4,2560]{2,1,0:T(4,128)(2,1)}) %all-gather.5.cloned.1.call-update) | async-done | bytes 2621456 | tf_op jit(solution)/shard_map/all_gather | solution.py:140
  57.1 5.3 %reshape.218 = bf16[512,2560]{1,0:T(8,128)(2,1)} reshape(bf16[128,4,2560]{2,1,0:T(4,128)(2,1)} %all-gather.5.cloned.1.call-done) | data formatting | bytes 5242880 | tf_op jit(solution)/shard_map/reshape | solution.py:141
  62.5 3.4 convolution_convert_fusion.1
  67.4 8.5 %convolution_convert_fusion = bf16[512,2048]{1,0:T(8,128)(2,1)S(1)} fusion(bf16[512,2560]{1,0:T(8,128)(2,1)S(1)} %copy-done.4, bf16[2560,2048]{1,0:T(8,128)(2,1)} %param.13), kind=kOutput, calls=%fused_computation.13 | convolution fusion | flops 5369757696 | bytes 15204352 | tf_op jit(solution)/shard_map/dot_general | solution.py:143
  76.2 2.7 convert_element_type.73
  82.3 12.3 %reshape.220 = bf16[50,128,4,128]{3,2,1,0:T(4,128)(2,1)} reshape(bf16[50,128,512]{2,1,0:T(8,128)(2,1)} %param.20) | data formatting | bytes 13107200 | tf_op jit(solution)/shard_map/reshape | solution.py:130
  94.6 12.4 %reshape.221 = bf16[50,128,4,128]{3,2,1,0:T(4,128)(2,1)} reshape(bf16[50,128,512]{2,1,0:T(8,128)(2,1)} %param.21) | data formatting | bytes 13107200 | tf_op jit(solution)/shard_map/reshape | solution.py:131
  113.7 2.3 reshape.259
  121.6 6.8 %select_reduce_fusion.1 = (f32[50,4,4,4]{3,2,1,0:T(4,128)S(1)}, f32[50,4,4,4,128]{4,3,2,1,0:T(4,128)S(1)}) fusion(pred[50,4,128]{2,1,0:T(4,128)(4,1)S(1)} %or_and_fusion, bf16[50,4,4,4,128]{4,3,1,2,0:T(4,128)(2,1)} %gather_fusion.1, bf16[50,128,4,128,1]{3,2,1,0,4:T(4,128)(2,1)} %bitcast.71), kind=kOutput, calls=%fused_computation.28 | convolution fusion | flops 106083200 | bytes 9049600 | tf_op jit(solution)/shard_map/nsagh,nbah->nasgb/dot_general | solution.py:37
  129.5 49.1 %pmax.7 = f32[64,4,4,4]{0,3,2,1:T(4,128)S(1)} all-reduce(f32[64,4,4,4]{0,3,2,1:T(4,128)S(1)} %select_reduce_fusion), channel_id=1, replica_groups=mesh['row'=2,'col'=2,'seq'=8] {'seq'}, use_global_device_ids=true, to_apply=%region_5.6 | all-reduce | flops 4096 | bytes 32768 | tf_op jit(solution)/shard_map/pmax | solution.py:173
  178.7 2.8 fusion.23
  183.8 4.8 %fusion.20 = f32[50,4,4,4,128]{4,3,2,1,0:T(4,128)S(1)} fusion(bf16[50,128,4,128,1]{3,2,1,0,4:T(4,128)(2,1)} %bitcast.70, f32[50,4,4,4,128]{4,3,2,1,0:T(4,128)} %copy-done.5, f32[50,4,4,4]{3,2,1,0:T(4,128)S(1)} %bitcast.78, f32[50,4,4,4]{3,2,1,0:T(4,128)S(1)} %get-tuple-element.41, pred[50,4,128]{2,1,0:T(4,128)(4,1)S(1)} %copy-done.17), kind=kOutput, calls=%fused_computation.31 | convolution fusion | flops 106905600 | bytes 9881600 | tf_op jit(solution)/shard_map/nasgb,nbah->nasgh/dot_general | solution.py:54
  188.6 3.2 fusion.17
  196.5 9.3 %fusion.32 = f32[64,4,4,4,4]{3,4,2,1,0:T(4,128)S(1)} fusion(bf16[64,4,4,4,128]{4,3,2,0,1:T(4,128)(2,1)S(1)} %pad_maximum_fusion.1, bf16[64,4,4,64]{3,1,2,0:T(4,128)(2,1)S(1)} %get-tuple-element.31, bf16[64,4,4,64]{3,1,2,0:T(4,128)(2,1)S(1)} %get-tuple-element.30), kind=kOutput, calls=%fused_computation.49 | convolution fusion | flops 4718592 | bytes 1376256 | tf_op jit(solution)/shard_map/rsagh,ruah->rasgu/dot_general | solution.py:83
  210.0 33.9 %psum.15 = bf16[64,4,4,4]{0,3,2,1:T(4,128)(2,1)S(1)} all-reduce(bf16[64,4,4,4]{0,3,2,1:T(4,128)(2,1)S(1)} %convert_element_type.84), channel_id=1, replica_groups=mesh['row'=2,'col'=2,'seq'=8] {'seq'}, use_global_device_ids=true, to_apply=%region_9.10 | all-reduce | flops 4096 | bytes 16384 | tf_op jit(solution)/shard_map/psum | solution.py:176
  245.5 68.4 %all-gather.9.cloned.1.call-done = bf16[512,4,4,4,128]{4,0,3,2,1:T(8,128)(2,1)} async-done(((bf16[64,4,4,4,128]{4,0,3,2,1:T(8,128)(2,1)}), bf16[512,4,4,4,128]{4,0,3,2,1:T(8,128)(2,1)}) %all-gather.9.cloned.1.call-update) | async-done | bytes 8388624 | tf_op jit(solution)/shard_map/all_gather | solution.py:177
  313.9 5.7 %reduce_sum.40 = bf16[64,4,4,4,128]{4,0,3,2,1:T(8,128)(2,1)S(1)} reduce(bf16[8,64,4,4,4,128]{5,1,0,4,3,2:T(8,128)(2,1)} %bitcast.69, bf16[]{:T(256)} %constant.35.clone.1), dimensions={0}, to_apply=%region_6.7 | reduce | flops 3670016 | bytes 9437186 | tf_op jit(solution)/shard_map/reduce_sum | solution.py:177
  324.2 8.7 %all-gather.7.cloned.1.call-done = bf16[128,4,2048]{2,0,1:T(8,128)(2,1)} async-done(((bf16[64,4,2048]{2,0,1:T(8,128)(2,1)}), bf16[128,4,2048]{2,0,1:T(8,128)(2,1)}) %all-gather.7.cloned.1.call-update) | async-done | bytes 2097168 | tf_op jit(solution)/shard_map/all_gather | solution.py:191
  332.8 10.0 %fusion.6 = bf16[128,4,2560]{2,0,1:T(8,128)(2,1)} fusion(bf16[128,4,2048]{2,0,1:T(8,128)(2,1)} %all-gather.7.cloned.1.call-done, bf16[2048,2560]{1,0:T(8,128)(2,1)} %param.16), kind=kOutput, calls=%fused_computation.9 | convolution fusion | flops 5370019840 | bytes 15204352 | tf_op jit(solution)/shard_map/dot_general | solution.py:193
  345.0 36.8 %reduce-scatter.2.cloned.1.call-done = bf16[64,4,2560]{2,0,1:T(8,128)(2,1)} async-done(((bf16[128,4,2560]{2,0,1:T(8,128)(2,1)}), bf16[64,4,2560]{2,0,1:T(8,128)(2,1)}) %reduce-scatter.2.cloned.1.call-update) | async-done | bytes 1310736 | tf_op jit(solution)/shard_map/reduce_scatter | solution.py:197
  381.8 3.4 copy.167
  (110 shorter events, 37.5 us)
Async XLA Ops:
  7.2 55.3 %copy-start = (bf16[2560,512]{1,0:T(8,128)(2,1)S(1)}, bf16[2560,512]{1,0:T(8,128)(2,1)}, u32[]{:S(2)}) copy-start(bf16[2560,512]{1,0:T(8,128)(2,1)} %param.15) | copy-start | bytes 7864324
  7.2 50.0 %all-gather.5.cloned.1.call-start = ((), (), s32[]{:S(2)}) async-start(), calls=%async_computation.1 | async-start | bytes 3932160 | tf_op jit(solution)/shard_map/all_gather | solution.py:140
  15.4 93.3 %all-reduce.3.cloned.1.call-start = ((), (), s32[]{:S(2)}) async-start(), calls=%async_computation.5 | async-start | bytes 6291456
  62.4 3.4 copy-start.4
  62.4 3.4 copy-start.22
  78.9 234.9 %all-gather.9.cloned.1.call-start = ((), (), s32[]{:S(2)}) async-start(), calls=%async_computation.4 | async-start | bytes 9437184 | tf_op jit(solution)/shard_map/all_gather | solution.py:177
  94.6 12.4 %copy-start.24 = (u32[32]{0:T(128)S(1)}, u32[32]{0:T(128)}, u32[]{:S(2)}) copy-start(u32[32]{0:T(128)} %constant.42) | copy-start | bytes 388
  94.6 13.6 %copy-start.23 = (s32[50]{0:T(128)S(1)}, s32[50]{0:T(128)}, u32[]{:S(2)}) copy-start(s32[50]{0:T(128)} %param.19) | copy-start | bytes 604
  108.7 70.0 %copy-start.16 = (pred[50,4,128]{2,1,0:T(4,128)(4,1)}, pred[50,4,128]{2,1,0:T(4,128)(4,1)S(1)}, u32[]{:S(2)}) copy-start(pred[50,4,128]{2,1,0:T(4,128)(4,1)S(1)} %or_and_fusion) | copy-start | bytes 76804
  110.5 1.6 copy-start.3
  128.4 50.2 %copy-start.5 = (f32[50,4,4,4,128]{4,3,2,1,0:T(4,128)}, f32[50,4,4,4,128]{4,3,2,1,0:T(4,128)S(1)}, u32[]{:S(2)}) copy-start(f32[50,4,4,4,128]{4,3,2,1,0:T(4,128)S(1)} %get-tuple-element.42) | copy-start | bytes 4915204
  178.6 5.1 %copy-start.14 = (f32[64,4,4,4]{0,3,2,1:T(4,128)}, f32[64,4,4,4]{0,3,2,1:T(4,128)S(1)}, u32[]{:S(2)}) copy-start(f32[64,4,4,4]{0,3,2,1:T(4,128)S(1)} %pmax.7) | copy-start | bytes 49156
  181.5 2.3 copy-start.17
  183.7 4.8 %copy-start.19 = (s32[50]{0:T(128)S(1)}, s32[50]{0:T(128)}, u32[]{:S(2)}) copy-start(s32[50]{0:T(128)} %param.18) | copy-start | bytes 604
  188.5 6.7 %copy-start.7 = (f32[64,4,64]{2,1,0:T(4,128)S(1)}, f32[64,4,64]{2,1,0:T(4,128)}, u32[]{:S(2)}) copy-start(f32[64,4,64]{2,1,0:T(4,128)} %copy-done.6) | copy-start | bytes 196612
  188.5 6.7 %copy-start.9 = (f32[64,4,64]{2,1,0:T(4,128)S(1)}, f32[64,4,64]{2,1,0:T(4,128)}, u32[]{:S(2)}) copy-start(f32[64,4,64]{2,1,0:T(4,128)} %copy-done.8) | copy-start | bytes 196612
  191.8 141.1 %all-gather.7.cloned.1.call-start = ((), (), s32[]{:S(2)}) async-start(), calls=%async_computation.2 | async-start | bytes 3145728 | tf_op jit(solution)/shard_map/all_gather | solution.py:191
  205.8 1.3 copy-start.21
  205.8 3.9 copy-start.20
  205.8 38.0 %copy-start.15 = (f32[64,4,4,4]{0,3,2,1:T(4,128)S(1)}, f32[64,4,4,4]{0,3,2,1:T(4,128)}, u32[]{:S(2)}) copy-start(f32[64,4,4,4]{0,3,2,1:T(4,128)} %copy-done.14) | copy-start | bytes 49156
  323.9 57.9 %reduce-scatter.2.cloned.1.call-start = ((), (), s32[]{:S(2)}) async-start(), calls=%async_computation.3 | async-start | bytes 3932160 | tf_op jit(solution)/shard_map/reduce_scatter | solution.py:197
  342.9 0.9 copy-start.11
  342.9 1.0 copy-start.13
  343.9 41.3 %copy-start.1 = (bf16[2560,512]{1,0:T(8,128)(2,1)S(1)}, bf16[2560,512]{1,0:T(8,128)(2,1)}, u32[]{:S(2)}) copy-start(bf16[2560,512]{1,0:T(8,128)(2,1)} %param.15) | copy-start | bytes 7864324
  (6 other events, 4.2 us)
Sparse Core Ops, SparseCore 0:
  15.5 41.5 all-gather.4
  79.1 23.2 all-reduce.2
  191.9 121.9 all-gather.8
  324.0 8.7 all-gather.6
  343.0 38.7 reduce-scatter.1
